TPU v7x, 128 devices: a whole 4x4x4 slice. The times are simulated.
128 devices in a mesh: seq: 32 (over x, y, core), fsdp: 4 (over z).
Axes of the slice: x: 4, y: 4, z: 4, core: 2. Of those that a mesh axis runs over, the one named last changes fastest.
Arguments:
- patches: bfloat16 [32768, 1280], P(('seq', 'fsdp')), may hold values from -6 to 6
- vis_index: int32 [32768], P(('seq', 'fsdp')), may hold values from 0 to 131071, as said below
- kv_list: int32 [256, 16], P(('seq', 'fsdp')), may hold values from 0 to 255, as said below
- kv_count: int32 [256], P(('seq', 'fsdp')), may hold values from 1 to 16, as said below
- global_tiles: int32 [2], replicated, may hold values from 0 to 255
- frame_table: bfloat16 [256, 1280], replicated, may hold values from -3 to 3
- space_table: bfloat16 [512, 1280], replicated, may hold values from -3 to 3
- ln_gain: bfloat16 [1280], replicated, may hold values from 0.25 to 1.75
- ln_bias: bfloat16 [1280], replicated, may hold values from -3 to 3
- w_qkv: bfloat16 [1280, 3840], P('fsdp')
- w_out: bfloat16 [1280, 1280], P('fsdp'), may hold values from -1.25 to 1.25
Outputs:
- attended: bfloat16 [32768, 1280], P(('seq', 'fsdp'))
Inputs may be any that keep to these rules, and one draw needn't show every extreme that they name: `vis_index`: exactly one visible position in each aligned group of four; strictly increasing. `kv_list`: the first entry of query tile i is i itself; entries may repeat; every entry t satisfies |t // 8 - i // 8| <= 2. Over all entries of an aligned run of 2 query tiles, the tiles that lie in any one group other than the run's own group (group = tile // 8) number at most 3 distinct ones, and exactly 3 for every such group within two of the run's own. On every device at least one query tile has kv_count = 16.
All inputs are finite; a program needn't handle non-finite values.
Results may differ from a plain program's by a relative error of at most 0.0065.
Values may be sent and summed in bfloat16 or wider, within the bound.
No kernel may reach another device: no remote copies, remote signals or barrier semaphores. Data moves between devices by JAX's collectives and lax.ppermute only.
A program may use at most 192 MiB of HBM per device.

v0:
```python
import jax
import jax.numpy as jnp
from jax import lax
from jax.sharding import PartitionSpec as P

HEADS = 16
TILE = 128
KT = 16
GLOBAL = 2
PATCHES = 512
NEAR = 3
REACH = (-2, -1, 1, 2)


def passed_along(block, axis, distance):
    devices = range(lax.axis_size(axis))
    route = [(i - distance, i) for i in devices if i - distance in devices]
    return lax.ppermute(block, axis, route)


def layer_norm(stream, ln_gain, ln_bias):
    stream32 = stream.astype(jnp.float32)
    mean_val = jnp.mean(stream32, axis=-1, keepdims=True)
    centred = stream32 - mean_val
    variance = jnp.mean(centred * centred, axis=-1, keepdims=True)
    scaled = centred * lax.rsqrt(variance + 1e-06)
    return (scaled * ln_gain.astype(jnp.float32) + ln_bias.astype(jnp.float32)).astype(jnp.bfloat16)


def embed(patches, vis_index, frame_table, space_table):
    frame_ids = vis_index // PATCHES
    patch_ids = vis_index % PATCHES
    return (
        patches.astype(jnp.float32)
        + frame_table[frame_ids].astype(jnp.float32)
        + space_table[patch_ids].astype(jnp.float32)
    ).astype(jnp.bfloat16)


def near_tiles(entries, group, group_tiles):
    cand = group * group_tiles + jnp.arange(group_tiles, dtype=jnp.int32)
    named = jnp.any(entries.reshape(-1, 1) == cand[None, :], axis=0)
    rank = jnp.cumsum(named.astype(jnp.int32)) - 1
    local_ids = jnp.arange(group_tiles, dtype=jnp.int32)
    picks = jnp.stack([jnp.sum(jnp.where(named & (rank == j), local_ids, 0)) for j in range(NEAR)])
    return (picks, rank)


def attend_tile(query_tile, key_values, key_live, feat_width):
    head_size = feat_width // HEADS
    key_rows = key_values.shape[0]
    queries_h = query_tile.reshape(TILE, HEADS, head_size)
    keys_h = key_values[:, :feat_width].reshape(key_rows, HEADS, head_size)
    values_h = key_values[:, feat_width:].reshape(key_rows, HEADS, head_size)
    scores = jnp.einsum(
        "qhd,khd->hqk", queries_h, keys_h, preferred_element_type=jnp.float32
    ) * head_size ** (-0.5)
    scores = jnp.where(key_live[None, None, :], scores, -jnp.inf)
    row_max = jnp.max(scores, axis=-1, keepdims=True)
    weights_raw = jnp.exp(scores - row_max)
    probs = (weights_raw / jnp.sum(weights_raw, axis=-1, keepdims=True)).astype(jnp.bfloat16)
    mixed_h = jnp.einsum("hqk,khd->qhd", probs, values_h, preferred_element_type=jnp.float32)
    return mixed_h.reshape(TILE, feat_width).astype(jnp.bfloat16)


def local(
    patches,
    vis_index,
    kv_list,
    kv_count,
    global_tiles,
    frame_table,
    space_table,
    ln_gain,
    ln_bias,
    w_qkv,
    w_out,
):
    tok_rows = patches.shape[0]
    feat_width = patches.shape[1]
    tile_count = tok_rows // TILE
    fsdp_size = lax.axis_size("fsdp")
    seq_size = lax.axis_size("seq")
    seq_at = lax.axis_index("seq")
    dev_at = seq_at * fsdp_size + lax.axis_index("fsdp")
    group_tiles = tile_count * fsdp_size
    stream = embed(patches, vis_index, frame_table, space_table)
    global_rows = []
    for slot_no in range(GLOBAL):
        tile_id = global_tiles[slot_no]
        mine = tile_id // tile_count == dev_at
        rows = lax.dynamic_slice_in_dim(stream, tile_id % tile_count * TILE, TILE, 0)
        global_rows.append(jnp.where(mine, rows, jnp.zeros_like(rows)))
    global_stream = lax.psum(jnp.concatenate(global_rows, axis=0), ("seq", "fsdp"))
    w_full = lax.all_gather(w_qkv, "fsdp", axis=0, tiled=True)
    normed = layer_norm(stream, ln_gain, ln_bias)
    qkv = jnp.dot(normed, w_full, preferred_element_type=jnp.float32).astype(jnp.bfloat16)
    query = qkv[:, :feat_width]
    keyval = qkv[:, feat_width:]
    global_normed = layer_norm(global_stream, ln_gain, ln_bias)
    global_kv = (
        jnp.dot(global_normed, w_full[:, feat_width:], preferred_element_type=jnp.float32)
        .astype(jnp.bfloat16)
        .reshape(GLOBAL, TILE, 2 * feat_width)
    )
    group_block = lax.all_gather(keyval, "fsdp", axis=0, tiled=True).reshape(
        group_tiles, TILE, 2 * feat_width
    )
    seq_lists = lax.all_gather(kv_list, "seq", axis=0, tiled=True)
    near_blocks = []
    near_rank = []
    for reach in REACH:
        distance = -reach
        dest = jnp.clip(seq_at + distance, 0, seq_size - 1)
        dest_lists = lax.dynamic_slice_in_dim(seq_lists, dest * tile_count, tile_count, 0)
        send_ids, unused = near_tiles(dest_lists, seq_at, group_tiles)
        sent = passed_along(group_block[send_ids], "seq", distance)
        near_blocks.append(sent)
        unused2, rank = near_tiles(kv_list, seq_at + reach, group_tiles)
        near_rank.append(rank)
    window = jnp.concatenate([group_block] + near_blocks + [global_kv], axis=0)
    near_rank = jnp.stack(near_rank)
    entry_group = kv_list // group_tiles
    entry_local = kv_list % group_tiles
    reach_of = entry_group - seq_at
    reach_slot = jnp.where(reach_of < 0, reach_of + 2, reach_of + 1)
    reach_slot = jnp.clip(reach_slot, 0, len(REACH) - 1)
    entry_rank = near_rank[reach_slot, entry_local]
    local_lists = jnp.where(
        reach_of == 0, entry_local, group_tiles + NEAR * reach_slot + entry_rank
    )
    global_slots = group_tiles + NEAR * len(REACH) + jnp.arange(GLOBAL, dtype=jnp.int32)
    query_tiles = query.reshape(tile_count, TILE, feat_width)

    def per_tile(tile_args):
        query_tile, local_ids, live_count = tile_args
        slot_live_row = jnp.concatenate(
            [jnp.arange(KT) < live_count, jnp.ones((GLOBAL,), dtype=bool)]
        )
        key_live = jnp.repeat(slot_live_row, TILE)
        key_values = window[jnp.concatenate([local_ids, global_slots])].reshape(
            (KT + GLOBAL) * TILE, 2 * feat_width
        )
        return attend_tile(query_tile, key_values, key_live, feat_width)

    heads_out = lax.map(per_tile, (query_tiles, local_lists, kv_count)).reshape(
        tok_rows, feat_width
    )
    return jnp.dot(
        heads_out,
        lax.all_gather(w_out, "fsdp", axis=0, tiled=True),
        preferred_element_type=jnp.float32,
    ).astype(jnp.bfloat16)


def solution(mesh):
    return jax.shard_map(
        local,
        mesh=mesh,
        in_specs=(
            P(("seq", "fsdp"), None),
            P(("seq", "fsdp")),
            P(("seq", "fsdp"), None),
            P(("seq", "fsdp")),
            P(),
            P(),
            P(),
            P(),
            P(),
            P("fsdp", None),
            P("fsdp", None),
        ),
        out_specs=P(("seq", "fsdp"), None),
        check_vma=False,
    )
```

profile of v0, /device:TPU:28, one launch (start us, length us, event | category | flops | bytes accessed | tf_op | source)
XLA Modules:
  0.0 548.4 jit_solution(2590682510310247328)
XLA Ops:
  10.2 1.3 gather_fusion.2
  11.5 1.2 gather_fusion.3
  13.5 93.8 %all-gather.5.cloned.1.call-done = bf16[1280,3840]{1,0:T(8,128)(2,1)} async-done(((bf16[320,3840]{1,0:T(8,128)(2,1)}), bf16[1280,3840]{1,0:T(8,128)(2,1)}) %all-gather.5.cloned.1.call-update) | async-done | bytes 9830416 | tf_op jit(solution)/shard_map/all_gather | solution.py:95
  107.2 6.6 %convolution_convert_fusion = bf16[256,3840]{1,0:T(8,128)(2,1)S(1)} fusion(bf16[1280,3840]{1,0:T(8,128)(2,1)} %all-gather.5.cloned.1.call-done, bf16[256,1280]{1,0:T(8,128)(2,1)S(1)} %get-tuple-element.114, f32[1280]{0:T(1024)S(1)} %convert_element_type.182, f32[1280]{0:T(1024)S(1)} %convert_element_type.181, f32[256]{0:T(256)S(1)} %add_rsqrt_fusion.1, ...), kind=kOutput, calls=%fused_computation.34 | convolution fusion | flops 2519531520 | bytes 12464128 | tf_op jit(solution)/shard_map/dot_general | solution.py:97
  113.9 1.2 copy-done.4
  115.2 1.2 slice.46
  122.4 0.9 pad_maximum_fusion
  124.1 22.4 %all-gather = s32[32,2,16]{2,1,0:T(2,128)S(1)} all-gather(s32[1,2,16]{2,1,0:T(2,128)S(1)} %bitcast.181), channel_id=1, replica_groups=mesh['seq'=32,'fsdp'=4] {'seq'}, dimensions={0}, use_global_device_ids=true | all-gather | bytes 4224 | tf_op jit(solution)/shard_map/all_gather | solution.py:109
  147.3 0.7 fusion.65
  148.2 0.7 fusion.68
  148.9 3.8 fusion.61
  152.9 0.7 fusion.71
  153.9 0.7 fusion.74
  154.6 3.8 fusion.63
  159.5 0.8 gather_fusion.1
  160.4 14.5 %all-gather.7.cloned.1.call-done = bf16[1024,2560]{1,0:T(8,128)(2,1)} async-done(((bf16[256,2560]{1,0:T(8,128)(2,1)}), bf16[1024,2560]{1,0:T(8,128)(2,1)}) %all-gather.7.cloned.1.call-update) | async-done | bytes 5242896 | tf_op jit(solution)/shard_map/all_gather | solution.py:106
  174.9 4.6 gather_fusion.4
  179.5 3.0 collective-permute-start
  182.5 137.3 %all-reduce.3.cloned.1.call-done = bf16[256,1280]{1,0:T(8,128)(2,1)} async-done(((bf16[256,1280]{1,0:T(8,128)(2,1)}), bf16[256,1280]{1,0:T(8,128)(2,1)}) %all-reduce.3.cloned.1.call-update) | async-done | bytes 655376 | tf_op jit(solution)/shard_map/psum | solution.py:94
  319.8 1.3 convert_reduce_fusion
  321.2 4.5 gather_fusion.5
  325.7 2.1 collective-permute-start.1
  328.1 4.6 gather_fusion.6
  332.7 3.4 collective-permute-start.2
  336.2 4.7 gather_fusion.7
  340.9 2.6 collective-permute-start.3
  343.5 4.8 fusion.17
  348.7 1.7 constant_dynamic-update-slice_fusion.5
  350.4 1.6 collective-permute-done.1
  351.9 1.7 constant_dynamic-update-slice_fusion.4
  353.6 19.3 %collective-permute-done.2 = bf16[3,128,2560]{2,1,0:T(8,128)(2,1)} collective-permute-done((bf16[3,128,2560]{2,1,0:T(8,128)(2,1)}, bf16[3,128,2560]{2,1,0:T(8,128)(2,1)}, u32[]{:S(2)}, u32[]{:S(2)}) %collective-permute-start.2) | collective-permute-done | bytes 1966112 | tf_op jit(solution)/shard_map/ppermute | solution.py:18
  373.0 1.7 constant_dynamic-update-slice_fusion.3
  374.7 30.7 %collective-permute-done.3 = bf16[3,128,2560]{2,1,0:T(8,128)(2,1)S(1)} collective-permute-done((bf16[3,128,2560]{2,1,0:T(8,128)(2,1)}, bf16[3,128,2560]{2,1,0:T(8,128)(2,1)S(1)}, u32[]{:S(2)}, u32[]{:S(2)}) %collective-permute-start.3) | collective-permute-done | bytes 1966112 | tf_op jit(solution)/shard_map/ppermute | solution.py:18
  405.6 5.0 copy-done.2
  410.6 126.7 %while.11 = (s32[]{:T(128)}, bf16[2,128,1280]{2,1,0:T(8,128)(2,1)S(1)}, s32[2,16]{1,0:T(2,128)S(1)}, bf16[22,128,2560]{2,1,0:T(8,128)(2,1)}, s32[2]{0:T(128)S(1)...) while((s32[]{:T(128)}, bf16[2,128,1280]{2,1,0:T(8,128)(2,1)S(1)}, ...), condition=%wide.region_36.37_spmd.clone, body=%wide.region_33.36_spmd.clone.sunk | while | flops 1538428160 | bytes 123626584 | solution.py:146
  410.7 11.3 %gather_fusion = bf16[18,128,2560]{2,1,0:T(8,128)(2,1)} fusion(bf16[22,128,2560]{2,1,0:T(8,128)(2,1)} %get-tuple-element.205, s32[1024]{0:T(1024)S(1)} %pad_clamp_fusion.8), kind=kCustom, calls=%fused_computation.clone.clone.1 | custom fusion | bytes 23593032 | tf_op jit(solution)/shard_map/while/body/eval_jaxpr/gather | solution.py:141
  422.0 9.7 %fusion.102 = (bf16[2304,1280]{1,0:T(8,128)(2,1)}, bf16[2304,1280]{1,0:T(8,128)(2,1)}) fusion(bf16[2304,2560]{1,0:T(8,128)(2,1)} %bitcast.166), kind=kLoop, calls=%fused_computation.186.clone.1 | loop fusion | bytes 23592960 | tf_op jit(solution)/shard_map/while/body/eval_jaxpr/slice | solution.py:53
  431.7 8.9 %copy.38 = bf16[2304,1280]{0,1:T(8,128)(2,1)} copy(bf16[2304,1280]{1,0:T(8,128)(2,1)} %get-tuple-element.183) | data formatting | bytes 11796480 | tf_op jit(solution)/shard_map/while
  442.1 11.3 %fusion.103 = (f32[16,128]{1,0:T(8,128)S(1)}, f32[16,128,2304]{2,1,0:T(8,128)}) fusion(pred[2304]{0:T(1024)(128)(4,1)S(1)} %broadcast_bitcast_fusion.2, bf16[128,16,80]{0,2,1:T(8,128)(2,1)S(1)} %bitcast.176, bf16[2304,16,80]{0,2,1:T(8,128)(2,1)} %bitcast.167), kind=kOutput, calls=%fused_computation.187.clone.1 | convolution fusion | flops 773851392 | bytes 25110784 | tf_op jit(solution)/shard_map/while/body/eval_jaxpr/sub | solution.py:60
  453.4 8.9 %copy.36 = bf16[2304,1280]{0,1:T(8,128)(2,1)} copy(bf16[2304,1280]{1,0:T(8,128)(2,1)} %get-tuple-element.182) | data formatting | bytes 11796480 | tf_op jit(solution)/shard_map/while
  462.2 11.5 %fusion.104 = bf16[16,80,128]{2,1,0:T(8,128)(2,1)S(1)} fusion(bf16[2304,16,80]{0,2,1:T(8,128)(2,1)} %bitcast.168, f32[16,128,2304]{2,1,0:T(8,128)} %get-tuple-element.184, f32[16,128]{1,0:T(8,128)S(1)} %get-tuple-element.185), kind=kOutput, calls=%fused_computation.19.clone.1 | convolution fusion | flops 764575744 | bytes 25108480 | tf_op jit(solution)/shard_map/while/body/eval_jaxpr/hqk,khd->qhd/dot_general | solution.py:62
  474.1 11.3 %gather_fusion = bf16[18,128,2560]{2,1,0:T(8,128)(2,1)} fusion(bf16[22,128,2560]{2,1,0:T(8,128)(2,1)} %get-tuple-element.205, s32[1024]{0:T(1024)S(1)} %pad_clamp_fusion.8), kind=kCustom, calls=%fused_computation.clone.clone.1 | custom fusion | bytes 23593032 | tf_op jit(solution)/shard_map/while/body/eval_jaxpr/gather | solution.py:141
  485.4 9.7 %fusion.102 = (bf16[2304,1280]{1,0:T(8,128)(2,1)}, bf16[2304,1280]{1,0:T(8,128)(2,1)}) fusion(bf16[2304,2560]{1,0:T(8,128)(2,1)} %bitcast.166), kind=kLoop, calls=%fused_computation.186.clone.1 | loop fusion | bytes 23592960 | tf_op jit(solution)/shard_map/while/body/eval_jaxpr/slice | solution.py:53
  495.0 8.9 %copy.38 = bf16[2304,1280]{0,1:T(8,128)(2,1)} copy(bf16[2304,1280]{1,0:T(8,128)(2,1)} %get-tuple-element.183) | data formatting | bytes 11796480 | tf_op jit(solution)/shard_map/while
  505.5 11.3 %fusion.103 = (f32[16,128]{1,0:T(8,128)S(1)}, f32[16,128,2304]{2,1,0:T(8,128)}) fusion(pred[2304]{0:T(1024)(128)(4,1)S(1)} %broadcast_bitcast_fusion.2, bf16[128,16,80]{0,2,1:T(8,128)(2,1)S(1)} %bitcast.176, bf16[2304,16,80]{0,2,1:T(8,128)(2,1)} %bitcast.167), kind=kOutput, calls=%fused_computation.187.clone.1 | convolution fusion | flops 773851392 | bytes 25110784 | tf_op jit(solution)/shard_map/while/body/eval_jaxpr/sub | solution.py:60
  516.7 8.9 %copy.36 = bf16[2304,1280]{0,1:T(8,128)(2,1)} copy(bf16[2304,1280]{1,0:T(8,128)(2,1)} %get-tuple-element.182) | data formatting | bytes 11796480 | tf_op jit(solution)/shard_map/while
  525.6 11.5 %fusion.104 = bf16[16,80,128]{2,1,0:T(8,128)(2,1)S(1)} fusion(bf16[2304,16,80]{0,2,1:T(8,128)(2,1)} %bitcast.168, f32[16,128,2304]{2,1,0:T(8,128)} %get-tuple-element.184, f32[16,128]{1,0:T(8,128)S(1)} %get-tuple-element.185), kind=kOutput, calls=%fused_computation.19.clone.1 | convolution fusion | flops 764575744 | bytes 25108480 | tf_op jit(solution)/shard_map/while/body/eval_jaxpr/hqk,khd->qhd/dot_general | solution.py:62
  537.4 3.9 convolution_convert_fusion.1
  (116 shorter events, 12.4 us)
Async XLA Ops:
  7.4 4.1 copy-start
  7.4 2.8 copy-start.3
  7.4 99.9 %all-gather.5.cloned.1.call-start = ((), (), s32[]{:S(2)}) async-start(), calls=%async_computation | async-start | bytes 12288000 | tf_op jit(solution)/shard_map/all_gather | solution.py:95
  8.1 166.8 %all-gather.7.cloned.1.call-start = ((), (), s32[]{:S(2)}) async-start(), calls=%async_computation.1 | async-start | bytes 6553600 | tf_op jit(solution)/shard_map/all_gather | solution.py:106
  11.5 1.3 copy-start.6
  113.9 1.3 copy-start.4
  115.1 1.2 copy-start.8
  116.3 7.7 %copy-start.7 = (s32[2,16]{1,0:T(2,128)S(1)}, s32[2,16]{1,0:T(2,128)}, u32[]{:S(2)}) copy-start(s32[2,16]{1,0:T(2,128)} %param.15) | copy-start | bytes 388
  116.3 203.5 %all-reduce.3.cloned.1.call-start = ((), (), s32[]{:S(2)}) async-start(), calls=%async_computation.2 | async-start | bytes 1310720 | tf_op jit(solution)/shard_map/psum | solution.py:94
  123.3 414.2 %all-gather.9.cloned.1.call-start = ((), (), s32[]{:S(2)}) async-start(), calls=%async_computation.3 | async-start | bytes 4096000 | tf_op jit(solution)/shard_map/all_gather | solution.py:151
  179.5 169.2 %collective-permute-start = (bf16[3,128,2560]{2,1,0:T(8,128)(2,1)}, bf16[3,128,2560]{2,1,0:T(8,128)(2,1)}, u32[]{:S(2)}, u32[]{:S(2)}) collective-permute-start(bf16[3,128,2560]{2,1,0:T(8,128)(2,1)} %gather_fusion.4), channel_id=1, source_target_pairs={{0,8},{4,12},{8,16},{12,20},{16,24},{20,28},{24,32},{28,36},{32,40... | collective-permute-start | bytes 5898248 | tf_op jit(solution)/shard_map/ppermute | solution.py:18
  319.8 8.0 %copy-start.5 = (bf16[256,1280]{1,0:T(8,128)(2,1)S(1)}, bf16[256,1280]{1,0:T(8,128)(2,1)}, u32[]{:S(2)}) copy-start(bf16[256,1280]{1,0:T(8,128)(2,1)} %all-reduce.3.cloned.1.call-done) | copy-start | bytes 1966084
  325.7 26.3 %collective-permute-start.1 = (bf16[3,128,2560]{2,1,0:T(8,128)(2,1)}, bf16[3,128,2560]{2,1,0:T(8,128)(2,1)}, u32[]{:S(2)}, u32[]{:S(2)}) collective-permute-start(bf16[3,128,2560]{2,1,0:T(8,128)(2,1)} %gather_fusion.5), channel_id=1, source_target_pairs={{0,4},{4,8},{8,12},{12,16},{16,20},{20,24},{24,28},{28,32},{32,36}... | collective-permute-start | bytes 5898248 | tf_op jit(solution)/shard_map/ppermute | solution.py:18
  332.7 40.3 %collective-permute-start.2 = (bf16[3,128,2560]{2,1,0:T(8,128)(2,1)}, bf16[3,128,2560]{2,1,0:T(8,128)(2,1)}, u32[]{:S(2)}, u32[]{:S(2)}) collective-permute-start(bf16[3,128,2560]{2,1,0:T(8,128)(2,1)} %gather_fusion.6), channel_id=1, source_target_pairs={{4,0},{8,4},{12,8},{16,12},{20,16},{24,20},{28,24},{32,28},{36,32}... | collective-permute-start | bytes 5898248 | tf_op jit(solution)/shard_map/ppermute | solution.py:18
  336.2 12.2 %slice-start = ((s8[5242880]{0:T(1024)(128)(4,1)}), s8[1048576]{0:T(1024)(128)(4,1)S(1)}, s32[]{:S(2)}) async-start(s8[5242880]{0:T(1024)(128)(4,1)} %bitcast.173), calls=%async_computation.4 | async-start | bytes 2097152
  340.9 7.5 %slice-start.1 = ((s8[5242880]{0:T(1024)(128)(4,1)}), s8[4194304]{0:T(1024)(128)(4,1)S(1)}, s32[]{:S(2)}) async-start(s8[5242880]{0:T(1024)(128)(4,1)} %bitcast.173), calls=%async_computation.5 | async-start | bytes 8388608
  340.9 64.5 %collective-permute-start.3 = (bf16[3,128,2560]{2,1,0:T(8,128)(2,1)}, bf16[3,128,2560]{2,1,0:T(8,128)(2,1)S(1)}, u32[]{:S(2)}, u32[]{:S(2)}) collective-permute-start(bf16[3,128,2560]{2,1,0:T(8,128)(2,1)} %gather_fusion.7), channel_id=1, source_target_pairs={{8,0},{12,4},{16,8},{20,12},{24,16},{28,20},{32,24},{36,28},{40,32... | collective-permute-start | bytes 5898248 | tf_op jit(solution)/shard_map/ppermute | solution.py:18
  374.6 36.0 %slice-start.2 = ((bf16[256,3840]{1,0:T(8,128)(2,1)}), bf16[256,1280]{1,0:T(8,128)(2,1)S(1)}, s32[]{:S(2)}) async-start(bf16[256,3840]{1,0:T(8,128)(2,1)} %copy-done.4), calls=%async_computation.6 | async-start | bytes 1310720 | tf_op jit(solution)/shard_map/slice | solution.py:98
  374.6 36.0 %copy-start.9 = (s32[2]{0:T(128)S(1)}, s32[2]{0:T(128)}, u32[]{:S(2)}) copy-start(s32[2]{0:T(128)} %param.16) | copy-start | bytes 28
  405.6 5.0 copy-start.2
  537.4 3.9 copy-start.1
Sparse Core Ops, SparseCore 0:
  9.8 97.3 all-gather.4
  116.5 58.4 all-gather.6
  176.6 41.3 all-gather.8
Sparse Core Ops, SparseCore 1:
  123.3 196.4 all-reduce.2
where the time goes:
time: 550 us; the launch traced here: 548 us
  waiting for transfers between devices  299 us (54%)
  local copies, waits for them, and re-layouts  115 us (21%)
  matrix products  61 us (11%)
  blocking collectives  22.4 us (4%)
  between operations  20.2 us (4%)
  other arithmetic  19.5 us (4%)
  starting transfers between devices  11.3 us (2%)
    psum x1, waiting for transfers between devices, local(): lax.psum(jnp.concatenate(global_rows, axis=0), ('seq', 'fsdp'))  137 us
    all_gather x1, waiting for transfers between devices, local(): w_full = lax.all_gather(w_qkv, 'fsdp', axis=0, tiled=True)  93.8 us
    ppermute x4, waiting for transfers between devices, passed_along(): return lax.ppermute(block, axis, route)  51.6 us
    while x4, local copies, waits for them, and re-layouts  35.4 us
    dot_general x2, matrix products, attend_tile(): jnp.einsum('hqk,khd->qhd', probs, values_h, preferred_element_type=jnp.fl...  23.1 us
    sub x2, matrix products, attend_tile(): weights_raw = jnp.exp(scores - row_max)  22.6 us
    gather x2, local copies, waits for them, and re-layouts, per_tile(): window[jnp.concatenate([local_ids, global_slots])]  22.5 us
    all_gather x1, blocking collectives, local(): seq_lists = lax.all_gather(kv_list, 'seq', axis=0, tiled=True)  22.4 us
  transfers between devices with their start and end apart: 8, of which 6 were waited for; matrix products, arithmetic and copies ran while one was open for 32% of the time, Pallas kernels for 0%

commit v1 on v0

--- a/solution.py
+++ b/solution.py
@@ -103,9 +103,39 @@
         .astype(jnp.bfloat16)
         .reshape(GLOBAL, TILE, 2 * feat_width)
     )
-    group_block = lax.all_gather(keyval, "fsdp", axis=0, tiled=True).reshape(
-        group_tiles, TILE, 2 * feat_width
-    )
+
+    def _store_ways(state):
+        tile_out, extra, z2 = (
+            lax.psum(1, axis_name="fsdp"),
+            lax.axis_index("fsdp"),
+            state.shape[0],
+        )
+        views = []
+        for num, u in enumerate(state.shape):
+            views.append(u * tile_out if num == 0 else u)
+        state_now = lax.dynamic_update_slice_in_dim(
+            jnp.zeros(views, state.dtype), state, extra * z2, axis=0
+        )
+        parts_out = z = state
+        for idx in tuple(range(1, tile_out // 2 + 1)):
+            store = []
+            for num in [*range(tile_out)]:
+                store.append((num, (num + 1) % tile_out))
+            parts_out = lax.ppermute(parts_out, axis_name="fsdp", perm=store)
+            state_now = lax.dynamic_update_slice_in_dim(
+                state_now, parts_out, (extra - idx) % tile_out * z2, axis=0
+            )
+            if 2 * idx < tile_out:
+                grid = []
+                for num in [*range(tile_out)]:
+                    grid.append((num, (num - 1) % tile_out))
+                z = lax.ppermute(z, axis_name="fsdp", perm=grid)
+                state_now = lax.dynamic_update_slice_in_dim(
+                    state_now, z, (extra + idx) % tile_out * z2, axis=0
+                )
+        return state_now
+
+    group_block = _store_ways(keyval).reshape(group_tiles, TILE, 2 * feat_width)
     seq_lists = lax.all_gather(kv_list, "seq", axis=0, tiled=True)
     near_blocks = []
     near_rank = []

time: 550 us -> 502 us (0.913)
  waiting for transfers between devices: 299 us -> 241 us
  local copies, waits for them, and re-layouts: 115 us -> 123 us
    psum x1, waiting for transfers between devices: 137 us -> 57.4 us  [local(): lax.psum(jnp.concatenate(global_rows, axis=0), ('seq', 'fsdp'))]
    ppermute x0 -> x3, waiting for transfers between devices: none -> 68.3 us  [the longest x2 68.3 us: _store_ways(): parts_out = lax.ppermute(parts_out, axis_name='fsdp', perm=store)]
    all_gather x1, waiting for transfers between devices: 93.8 us -> 62.4 us  [local(): w_full = lax.all_gather(w_qkv, 'fsdp', axis=0, tiled=True)]
    all_gather x1 -> x0, waiting for transfers between devices: 14.5 us -> none  [local(): lax.all_gather(keyval, 'fsdp', axis=0, tiled=True)]
    dynamic_update_slice x0 -> x3, local copies, waits for them, and re-layouts: none -> 6.13 us  [the longest x2 3.69 us: _store_ways(): lax.dynamic_update_slice_in_dim(state_now, parts_out, (extra - idx) % til...]
    unnamed x29 -> x35, local copies, waits for them, and re-layouts: 11.8 us -> 13.7 us
  transfers between devices with their start and end apart: 8 -> 10, of which waited for: 6 -> 7; matrix products, arithmetic and copies ran while one was open for 32% -> 38% of each run, Pallas kernels for 0% -> 0%
where the time goes in v1:
time: 502 us; the launch traced here: 501 us
  waiting for transfers between devices  241 us (48%)
  local copies, waits for them, and re-layouts  123 us (25%)
  matrix products  61.1 us (12%)
  blocking collectives  22.3 us (4%)
  between operations  20.3 us (4%)
  other arithmetic  17.8 us (4%)
  starting transfers between devices  14.4 us (3%)
    ppermute x2, waiting for transfers between devices, _store_ways(): parts_out = lax.ppermute(parts_out, axis_name='fsdp', perm=store)  68.3 us
    all_gather x1, waiting for transfers between devices, local(): w_full = lax.all_gather(w_qkv, 'fsdp', axis=0, tiled=True)  62.4 us
    psum x1, waiting for transfers between devices, local(): lax.psum(jnp.concatenate(global_rows, axis=0), ('seq', 'fsdp'))  57.4 us
    ppermute x4, waiting for transfers between devices, passed_along(): return lax.ppermute(block, axis, route)  51.7 us
    while x4, local copies, waits for them, and re-layouts  35.4 us
    dot_general x2, matrix products, attend_tile(): jnp.einsum('hqk,khd->qhd', probs, values_h, preferred_element_type=jnp.fl...  23.1 us
    sub x2, matrix products, attend_tile(): weights_raw = jnp.exp(scores - row_max)  22.6 us
    gather x2, local copies, waits for them, and re-layouts, per_tile(): window[jnp.concatenate([local_ids, global_slots])]  22.5 us
  transfers between devices with their start and end apart: 10, of which 7 were waited for; matrix products, arithmetic and copies ran while one was open for 38% of the time, Pallas kernels for 0%

profile of v1, /device:TPU:28, one launch (start us, length us, event | category | flops | bytes accessed | tf_op | source)
XLA Modules:
  0.0 500.7 jit_solution(375812454244328249)
XLA Ops:
  8.1 1.3 fusion.81
  15.1 1.3 gather_fusion.2
  16.4 1.2 gather_fusion.3
  20.4 22.3 %all-gather = s32[32,2,16]{2,1,0:T(2,128)S(1)} all-gather(s32[1,2,16]{2,1,0:T(2,128)S(1)} %bitcast.181), channel_id=1, replica_groups=mesh['seq'=32,'fsdp'=4] {'seq'}, dimensions={0}, use_global_device_ids=true | all-gather | bytes 4224 | tf_op jit(solution)/shard_map/all_gather | solution.py:139
  45.4 62.4 %all-gather.4.cloned.1.call-done = bf16[1280,3840]{1,0:T(8,128)(2,1)} async-done(((bf16[320,3840]{1,0:T(8,128)(2,1)}), bf16[1280,3840]{1,0:T(8,128)(2,1)}) %all-gather.4.cloned.1.call-update) | async-done | bytes 9830416 | tf_op jit(solution)/shard_map/all_gather | solution.py:95
  107.8 6.7 %convolution_convert_fusion = bf16[256,3840]{1,0:T(8,128)(2,1)S(1)} fusion(bf16[1280,3840]{1,0:T(8,128)(2,1)} %all-gather.4.cloned.1.call-done, bf16[256,1280]{1,0:T(8,128)(2,1)S(1)} %get-tuple-element.114, f32[1280]{0:T(1024)S(1)} %convert_element_type.182, f32[1280]{0:T(1024)S(1)} %convert_element_type.181, f32[256]{0:T(256)S(1)} %add_rsqrt_fusion.1, ...), kind=kOutput, calls=%fused_computation.34 | convolution fusion | flops 2519531520 | bytes 12464128 | tf_op jit(solution)/shard_map/dot_general | solution.py:97
  115.7 2.4 copy-done.3
  118.1 1.5 collective-permute-start
  120.4 1.8 collective-permute-start.1
  122.2 3.7 fusion.61
  128.6 47.9 %collective-permute-done = bf16[256,2560]{1,0:T(8,128)(2,1)} collective-permute-done((bf16[256,2560]{1,0:T(8,128)(2,1)S(1)}, bf16[256,2560]{1,0:T(8,128)(2,1)}, u32[]{:S(2)}, u32[]{:S(2)}) %collective-permute-start) | collective-permute-done | bytes 1310752 | tf_op jit(solution)/shard_map/ppermute | solution.py:124
  176.5 3.7 fusion.63
  180.2 2.5 constant_dynamic-update-slice_fusion.9
  182.7 2.4 constant_dynamic-update-slice_fusion.8
  185.2 20.4 %collective-permute-done.2 = bf16[256,2560]{1,0:T(8,128)(2,1)S(1)} collective-permute-done((bf16[256,2560]{1,0:T(8,128)(2,1)}, bf16[256,2560]{1,0:T(8,128)(2,1)S(1)}, u32[]{:S(2)}, u32[]{:S(2)}) %collective-permute-start.2) | collective-permute-done | bytes 1310752 | tf_op jit(solution)/shard_map/ppermute | solution.py:124
  205.5 1.2 constant_dynamic-update-slice_fusion.7
  206.8 4.6 gather_fusion.4
  211.3 3.0 collective-permute-start.3
  214.3 57.4 %all-reduce.3.cloned.1.call-done = bf16[256,1280]{1,0:T(8,128)(2,1)} async-done(((bf16[256,1280]{1,0:T(8,128)(2,1)}), bf16[256,1280]{1,0:T(8,128)(2,1)}) %all-reduce.3.cloned.1.call-update) | async-done | bytes 655376 | tf_op jit(solution)/shard_map/psum | solution.py:94
  271.7 1.3 convert_reduce_fusion
  273.1 4.5 gather_fusion.5
  277.6 2.1 collective-permute-start.4
  280.0 4.6 gather_fusion.6
  284.6 3.4 collective-permute-start.5
  288.1 4.7 gather_fusion.7
  292.8 2.5 collective-permute-start.6
  295.3 4.8 fusion.17
  300.5 1.7 constant_dynamic-update-slice_fusion.5
  302.2 1.7 collective-permute-done.4
  303.8 1.7 constant_dynamic-update-slice_fusion.4
  305.5 19.3 %collective-permute-done.5 = bf16[3,128,2560]{2,1,0:T(8,128)(2,1)} collective-permute-done((bf16[3,128,2560]{2,1,0:T(8,128)(2,1)}, bf16[3,128,2560]{2,1,0:T(8,128)(2,1)}, u32[]{:S(2)}, u32[]{:S(2)}) %collective-permute-start.5) | collective-permute-done | bytes 1966112 | tf_op jit(solution)/shard_map/ppermute | solution.py:18
  324.9 1.7 constant_dynamic-update-slice_fusion.3
  326.6 30.6 %collective-permute-done.6 = bf16[3,128,2560]{2,1,0:T(8,128)(2,1)S(1)} collective-permute-done((bf16[3,128,2560]{2,1,0:T(8,128)(2,1)}, bf16[3,128,2560]{2,1,0:T(8,128)(2,1)S(1)}, u32[]{:S(2)}, u32[]{:S(2)}) %collective-permute-start.6) | collective-permute-done | bytes 1966112 | tf_op jit(solution)/shard_map/ppermute | solution.py:18
  357.5 5.0 %copy-done.2 = bf16[22,128,2560]{2,1,0:T(8,128)(2,1)} copy-done((bf16[22,128,2560]{2,1,0:T(8,128)(2,1)}, bf16[22,128,2560]{2,1,0:T(8,128)(2,1)S(1)}, u32[]{:S(2)}) %copy-start.2) | copy-done | bytes 14417944
  362.5 126.8 %while.11 = (s32[]{:T(128)}, bf16[2,128,1280]{2,1,0:T(8,128)(2,1)S(1)}, s32[2,16]{1,0:T(2,128)S(1)}, bf16[22,128,2560]{2,1,0:T(8,128)(2,1)}, s32[2]{0:T(128)S(1)...) while((s32[]{:T(128)}, bf16[2,128,1280]{2,1,0:T(8,128)(2,1)S(1)}, ...), condition=%wide.region_36.37_spmd.clone, body=%wide.region_33.36_spmd.clone.sunk | while | flops 1538428160 | bytes 123626584 | solution.py:176
  362.7 11.3 %gather_fusion = bf16[18,128,2560]{2,1,0:T(8,128)(2,1)} fusion(bf16[22,128,2560]{2,1,0:T(8,128)(2,1)} %get-tuple-element.207, s32[1024]{0:T(1024)S(1)} %pad_clamp_fusion.8), kind=kCustom, calls=%fused_computation.clone.clone.1 | custom fusion | bytes 23593032 | tf_op jit(solution)/shard_map/while/body/eval_jaxpr/gather | solution.py:171
  373.9 9.7 %fusion.103 = (bf16[2304,1280]{1,0:T(8,128)(2,1)}, bf16[2304,1280]{1,0:T(8,128)(2,1)}) fusion(bf16[2304,2560]{1,0:T(8,128)(2,1)} %bitcast.166), kind=kLoop, calls=%fused_computation.190.clone.1 | loop fusion | bytes 23592960 | tf_op jit(solution)/shard_map/while/body/eval_jaxpr/slice | solution.py:53
  383.6 8.9 %copy.38 = bf16[2304,1280]{0,1:T(8,128)(2,1)} copy(bf16[2304,1280]{1,0:T(8,128)(2,1)} %get-tuple-element.185) | data formatting | bytes 11796480 | tf_op jit(solution)/shard_map/while
  394.0 11.3 %fusion.104 = (f32[16,128]{1,0:T(8,128)S(1)}, f32[16,128,2304]{2,1,0:T(8,128)}) fusion(pred[2304]{0:T(1024)(128)(4,1)S(1)} %broadcast_bitcast_fusion.2, bf16[128,16,80]{0,2,1:T(8,128)(2,1)S(1)} %bitcast.176, bf16[2304,16,80]{0,2,1:T(8,128)(2,1)} %bitcast.167), kind=kOutput, calls=%fused_computation.191.clone.1 | convolution fusion | flops 773851392 | bytes 25110784 | tf_op jit(solution)/shard_map/while/body/eval_jaxpr/sub | solution.py:60
  405.3 8.9 %copy.36 = bf16[2304,1280]{0,1:T(8,128)(2,1)} copy(bf16[2304,1280]{1,0:T(8,128)(2,1)} %get-tuple-element.184) | data formatting | bytes 11796480 | tf_op jit(solution)/shard_map/while
  414.1 11.5 %fusion.105 = bf16[16,80,128]{2,1,0:T(8,128)(2,1)S(1)} fusion(bf16[2304,16,80]{0,2,1:T(8,128)(2,1)} %bitcast.168, f32[16,128,2304]{2,1,0:T(8,128)} %get-tuple-element.186, f32[16,128]{1,0:T(8,128)S(1)} %get-tuple-element.187), kind=kOutput, calls=%fused_computation.19.clone.1 | convolution fusion | flops 764575744 | bytes 25108480 | tf_op jit(solution)/shard_map/while/body/eval_jaxpr/hqk,khd->qhd/dot_general | solution.py:62
  426.0 11.3 %gather_fusion = bf16[18,128,2560]{2,1,0:T(8,128)(2,1)} fusion(bf16[22,128,2560]{2,1,0:T(8,128)(2,1)} %get-tuple-element.207, s32[1024]{0:T(1024)S(1)} %pad_clamp_fusion.8), kind=kCustom, calls=%fused_computation.clone.clone.1 | custom fusion | bytes 23593032 | tf_op jit(solution)/shard_map/while/body/eval_jaxpr/gather | solution.py:171
  437.3 9.7 %fusion.103 = (bf16[2304,1280]{1,0:T(8,128)(2,1)}, bf16[2304,1280]{1,0:T(8,128)(2,1)}) fusion(bf16[2304,2560]{1,0:T(8,128)(2,1)} %bitcast.166), kind=kLoop, calls=%fused_computation.190.clone.1 | loop fusion | bytes 23592960 | tf_op jit(solution)/shard_map/while/body/eval_jaxpr/slice | solution.py:53
  447.0 8.9 %copy.38 = bf16[2304,1280]{0,1:T(8,128)(2,1)} copy(bf16[2304,1280]{1,0:T(8,128)(2,1)} %get-tuple-element.185) | data formatting | bytes 11796480 | tf_op jit(solution)/shard_map/while
  457.4 11.3 %fusion.104 = (f32[16,128]{1,0:T(8,128)S(1)}, f32[16,128,2304]{2,1,0:T(8,128)}) fusion(pred[2304]{0:T(1024)(128)(4,1)S(1)} %broadcast_bitcast_fusion.2, bf16[128,16,80]{0,2,1:T(8,128)(2,1)S(1)} %bitcast.176, bf16[2304,16,80]{0,2,1:T(8,128)(2,1)} %bitcast.167), kind=kOutput, calls=%fused_computation.191.clone.1 | convolution fusion | flops 773851392 | bytes 25110784 | tf_op jit(solution)/shard_map/while/body/eval_jaxpr/sub | solution.py:60
  468.7 8.9 %copy.36 = bf16[2304,1280]{0,1:T(8,128)(2,1)} copy(bf16[2304,1280]{1,0:T(8,128)(2,1)} %get-tuple-element.184) | data formatting | bytes 11796480 | tf_op jit(solution)/shard_map/while
  477.5 11.5 %fusion.105 = bf16[16,80,128]{2,1,0:T(8,128)(2,1)S(1)} fusion(bf16[2304,16,80]{0,2,1:T(8,128)(2,1)} %bitcast.168, f32[16,128,2304]{2,1,0:T(8,128)} %get-tuple-element.186, f32[16,128]{1,0:T(8,128)S(1)} %get-tuple-element.187), kind=kOutput, calls=%fused_computation.19.clone.1 | convolution fusion | flops 764575744 | bytes 25108480 | tf_op jit(solution)/shard_map/while/body/eval_jaxpr/hqk,khd->qhd/dot_general | solution.py:62
  489.3 3.9 convolution_convert_fusion.1
  (129 shorter events, 16.0 us)
Async XLA Ops:
  7.4 9.0 %copy-start = (bf16[512,1280]{1,0:T(8,128)(2,1)S(1)}, bf16[512,1280]{1,0:T(8,128)(2,1)}, u32[]{:S(2)}) copy-start(bf16[512,1280]{1,0:T(8,128)(2,1)} %param.19) | copy-start | bytes 3932164
  7.4 7.8 %copy-start.4 = (bf16[256,1280]{1,0:T(8,128)(2,1)S(1)}, bf16[256,1280]{1,0:T(8,128)(2,1)}, u32[]{:S(2)}) copy-start(bf16[256,1280]{1,0:T(8,128)(2,1)} %param.18) | copy-start | bytes 1966084
  7.4 100.4 %all-gather.4.cloned.1.call-start = ((), (), s32[]{:S(2)}) async-start(), calls=%async_computation | async-start | bytes 12288000 | tf_op jit(solution)/shard_map/all_gather | solution.py:95
  8.1 263.6 %all-reduce.3.cloned.1.call-start = ((), (), s32[]{:S(2)}) async-start(), calls=%async_computation.1 | async-start | bytes 1310720 | tf_op jit(solution)/shard_map/psum | solution.py:94
  16.4 1.3 copy-start.7
  17.7 2.5 copy-start.9
  17.7 2.6 copy-start.10
  17.7 2.6 copy-start.8
  19.1 470.2 %all-gather.6.cloned.1.call-start = ((), (), s32[]{:S(2)}) async-start(), calls=%async_computation.2 | async-start | bytes 4096000 | tf_op jit(solution)/shard_map/all_gather | solution.py:181
  114.5 1.3 copy-start.5
  115.7 2.4 copy-start.3
  118.1 58.4 %collective-permute-start = (bf16[256,2560]{1,0:T(8,128)(2,1)S(1)}, bf16[256,2560]{1,0:T(8,128)(2,1)}, u32[]{:S(2)}, u32[]{:S(2)}) collective-permute-start(bf16[256,2560]{1,0:T(8,128)(2,1)S(1)} %get-tuple-element.121), channel_id=1, source_target_pairs={{0,1},{1,2},{2,3},{3,0},{4,5},{5,6},{6,7},{7,4},{8,9},{9,10},{10,1... | collective-permute-start | bytes 3932168 | tf_op jit(solution)/shard_map/ppermute | solution.py:124
  120.4 62.3 %collective-permute-start.1 = (bf16[256,2560]{1,0:T(8,128)(2,1)S(1)}, bf16[256,2560]{1,0:T(8,128)(2,1)}, u32[]{:S(2)}, u32[]{:S(2)}) collective-permute-start(bf16[256,2560]{1,0:T(8,128)(2,1)S(1)} %get-tuple-element.121), channel_id=1, source_target_pairs={{0,3},{1,0},{2,1},{3,2},{4,7},{5,4},{6,5},{7,6},{8,11},{9,8},{10,9... | collective-permute-start | bytes 3932168 | tf_op jit(solution)/shard_map/ppermute | solution.py:132
  176.5 29.0 %collective-permute-start.2 = (bf16[256,2560]{1,0:T(8,128)(2,1)}, bf16[256,2560]{1,0:T(8,128)(2,1)S(1)}, u32[]{:S(2)}, u32[]{:S(2)}) collective-permute-start(bf16[256,2560]{1,0:T(8,128)(2,1)} %collective-permute-done), channel_id=1, source_target_pairs={{0,1},{1,2},{2,3},{3,0},{4,5},{5,6},{6,7},{7,4},{8,9},{9,10},{10,1... | collective-permute-start | bytes 3932168 | tf_op jit(solution)/shard_map/ppermute | solution.py:124
  211.3 89.2 %collective-permute-start.3 = (bf16[3,128,2560]{2,1,0:T(8,128)(2,1)}, bf16[3,128,2560]{2,1,0:T(8,128)(2,1)}, u32[]{:S(2)}, u32[]{:S(2)}) collective-permute-start(bf16[3,128,2560]{2,1,0:T(8,128)(2,1)} %gather_fusion.4), channel_id=1, source_target_pairs={{0,8},{4,12},{8,16},{12,20},{16,24},{20,28},{24,32},{28,36},{32,40... | collective-permute-start | bytes 5898248 | tf_op jit(solution)/shard_map/ppermute | solution.py:18
  271.7 8.0 %copy-start.6 = (bf16[256,1280]{1,0:T(8,128)(2,1)S(1)}, bf16[256,1280]{1,0:T(8,128)(2,1)}, u32[]{:S(2)}) copy-start(bf16[256,1280]{1,0:T(8,128)(2,1)} %all-reduce.3.cloned.1.call-done) | copy-start | bytes 1966084
  277.6 26.3 %collective-permute-start.4 = (bf16[3,128,2560]{2,1,0:T(8,128)(2,1)}, bf16[3,128,2560]{2,1,0:T(8,128)(2,1)}, u32[]{:S(2)}, u32[]{:S(2)}) collective-permute-start(bf16[3,128,2560]{2,1,0:T(8,128)(2,1)} %gather_fusion.5), channel_id=1, source_target_pairs={{0,4},{4,8},{8,12},{12,16},{16,20},{20,24},{24,28},{28,32},{32,36}... | collective-permute-start | bytes 5898248 | tf_op jit(solution)/shard_map/ppermute | solution.py:18
  284.6 40.3 %collective-permute-start.5 = (bf16[3,128,2560]{2,1,0:T(8,128)(2,1)}, bf16[3,128,2560]{2,1,0:T(8,128)(2,1)}, u32[]{:S(2)}, u32[]{:S(2)}) collective-permute-start(bf16[3,128,2560]{2,1,0:T(8,128)(2,1)} %gather_fusion.6), channel_id=1, source_target_pairs={{4,0},{8,4},{12,8},{16,12},{20,16},{24,20},{28,24},{32,28},{36,32}... | collective-permute-start | bytes 5898248 | tf_op jit(solution)/shard_map/ppermute | solution.py:18
  288.1 12.0 %slice-start = ((s8[5242880]{0:T(1024)(128)(4,1)}), s8[1048576]{0:T(1024)(128)(4,1)S(1)}, s32[]{:S(2)}) async-start(s8[5242880]{0:T(1024)(128)(4,1)} %bitcast.173), calls=%async_computation.3 | async-start | bytes 2097152
  292.8 7.4 %slice-start.1 = ((s8[5242880]{0:T(1024)(128)(4,1)}), s8[4194304]{0:T(1024)(128)(4,1)S(1)}, s32[]{:S(2)}) async-start(s8[5242880]{0:T(1024)(128)(4,1)} %bitcast.173), calls=%async_computation.4 | async-start | bytes 8388608
  292.8 64.5 %collective-permute-start.6 = (bf16[3,128,2560]{2,1,0:T(8,128)(2,1)}, bf16[3,128,2560]{2,1,0:T(8,128)(2,1)S(1)}, u32[]{:S(2)}, u32[]{:S(2)}) collective-permute-start(bf16[3,128,2560]{2,1,0:T(8,128)(2,1)} %gather_fusion.7), channel_id=1, source_target_pairs={{8,0},{12,4},{16,8},{20,12},{24,16},{28,20},{32,24},{36,28},{40,32... | collective-permute-start | bytes 5898248 | tf_op jit(solution)/shard_map/ppermute | solution.py:18
  326.5 36.0 %slice-start.2 = ((bf16[256,3840]{1,0:T(8,128)(2,1)}), bf16[256,1280]{1,0:T(8,128)(2,1)S(1)}, s32[]{:S(2)}) async-start(bf16[256,3840]{1,0:T(8,128)(2,1)} %copy-done.5), calls=%async_computation.5 | async-start | bytes 1310720 | tf_op jit(solution)/shard_map/slice | solution.py:98
  326.6 36.0 %copy-start.11 = (bf16[2,128,1280]{2,1,0:T(8,128)(2,1)S(1)}, bf16[2,128,1280]{2,1,0:T(8,128)(2,1)}, u32[]{:S(2)}) copy-start(bf16[2,128,1280]{2,1,0:T(8,128)(2,1)} %custom-call.17) | copy-start | bytes 1966084
  326.6 36.0 %copy-start.12 = (s32[2]{0:T(128)S(1)}, s32[2]{0:T(128)}, u32[]{:S(2)}) copy-start(s32[2]{0:T(128)} %param.16) | copy-start | bytes 28
  357.5 5.0 %copy-start.2 = (bf16[22,128,2560]{2,1,0:T(8,128)(2,1)}, bf16[22,128,2560]{2,1,0:T(8,128)(2,1)S(1)}, u32[]{:S(2)}) copy-start(bf16[22,128,2560]{2,1,0:T(8,128)(2,1)S(1)} %constant_dynamic-update-slice_fusion.1) | copy-start | bytes 43253764
  489.3 3.9 copy-start.1
Sparse Core Ops, SparseCore 0:
  9.8 97.8 all-gather.3
  109.4 67.3 all-gather.5
Sparse Core Ops, SparseCore 1:
  19.2 252.5 all-reduce.2
